TPU v7x, 512 devices: a whole 4x8x8 slice. The times are simulated.
512 devices in a mesh: wide: 32 (over z, x), tensor: 16 (over y, core).
Axes of the slice: x: 4, y: 8, z: 8, core: 2. Of those that a mesh axis runs over, the one named last changes fastest.
Arguments:
- tokens: bfloat16 [16384, 8192], P('wide', 'tensor'), may hold values from -6 to 6
- key_value_weight: bfloat16 [8192, 2048], P(None, 'tensor'), may hold values from -0.0625 to 0.0625
- adapter_down_maps: bfloat16 [8192, 512, 64], P('tensor', 'wide'), may hold values from -0.0625 to 0.0625
- adapter_up_maps: bfloat16 [512, 64, 2048], P('wide', None, 'tensor'), may hold values from -0.75 to 0.75
- adapter_per_row: int32 [16384], P('wide'), may hold values from 0 to 511, as said below
- adapter_storage_slot: int32 [512], replicated, may hold values from 0 to 511, as said below
Outputs:
- kv_out: bfloat16 [16384, 2048], P('wide', 'tensor')
Inputs may be any that keep to these rules, and one draw needn't show every extreme that they name: `adapter_per_row`: the adapter stored at position p belongs to owner p // 16 of wide. Among the 512 rows of one index of wide, at most 32 name adapters of one owner; in every draw one owner gets exactly 32 rows from every index of wide. `adapter_storage_slot`: each position is taken by exactly one adapter.
All inputs are finite; a program needn't handle non-finite values.
Results may differ from a plain program's by a relative error of at most 0.0049.
Values may be sent and summed in bfloat16 or wider, within the bound.
No kernel may reach another device: no remote copies, remote signals or barrier semaphores. Data moves between devices by JAX's collectives and lax.ppermute only.
A program may use at most 64 MiB of HBM per device.

v0:
```python
import jax
import jax.numpy as jnp
from jax import lax
from jax.sharding import PartitionSpec as P


def body(
    tokens,
    key_value_weight,
    adapter_down_maps,
    adapter_up_maps,
    adapter_per_row,
    adapter_storage_slot,
):
    row_count = tokens.shape[0]
    feature_portion = tokens.shape[1]
    wide_count = lax.axis_size("wide")
    capacity = 2 * row_count // wide_count
    present_adapters = adapter_down_maps.shape[1]
    rank_dimension = adapter_down_maps.shape[2]
    column_portion = key_value_weight.shape[1]
    gathered = lax.all_gather(tokens, "tensor", axis=1, tiled=True)
    base_projection_output = jnp.dot(gathered, key_value_weight, preferred_element_type=jnp.float32)
    total_adapters = adapter_storage_slot.shape[0]
    adapter_match = adapter_per_row[:, None] == jnp.arange(total_adapters, dtype=jnp.int32)[None, :]
    storage_position = jnp.sum(jnp.where(adapter_match, adapter_storage_slot[None, :], 0), axis=1)
    owner_index = storage_position // present_adapters
    local_index = storage_position % present_adapters
    owner_onehot = (
        owner_index[:, None] == jnp.arange(wide_count, dtype=jnp.int32)[None, :]
    ).astype(jnp.int32)
    earlier = jnp.cumsum(owner_onehot, axis=0) - owner_onehot
    rank_in_owner = jnp.sum(earlier * owner_onehot, axis=1)
    storage_slot_index = owner_index * capacity + rank_in_owner
    send_rows = (
        jnp.zeros((wide_count * capacity, feature_portion), jnp.bfloat16)
        .at[storage_slot_index]
        .set(tokens)
    )
    send_slots = (
        jnp.full((wide_count * capacity,), -1, jnp.int32).at[storage_slot_index].set(local_index)
    )
    send_rows = send_rows.reshape(wide_count, capacity, feature_portion)
    send_slots = send_slots.reshape(wide_count, capacity)
    down_matrix = adapter_down_maps.reshape(feature_portion, present_adapters * rank_dimension)
    up_matrix = adapter_up_maps.reshape(present_adapters * rank_dimension, column_portion)
    column_adapter = (
        jnp.arange(present_adapters * rank_dimension, dtype=jnp.int32) // rank_dimension
    )
    got_rows = lax.all_to_all(send_rows, "wide", split_axis=0, concat_axis=0, tiled=True)
    got_slots = lax.all_to_all(send_slots, "wide", split_axis=0, concat_axis=0, tiled=True)
    source_rows, entry_list = got_slots.shape
    flat_rows = got_rows.reshape(source_rows * entry_list, feature_portion)
    slot_adapter = got_slots.reshape(source_rows * entry_list)
    all_ranks = jnp.dot(flat_rows, down_matrix, preferred_element_type=jnp.float32)
    selected = slot_adapter[:, None] == column_adapter[None, :]
    partial_value = jnp.sum(
        jnp.where(selected, all_ranks, 0.0).reshape(
            source_rows * entry_list, present_adapters, rank_dimension
        ),
        axis=1,
    )
    summed = lax.psum(partial_value, "tensor")
    reduced_rows = summed.astype(jnp.bfloat16)
    expanded_rows = jnp.where(
        selected, jnp.tile(reduced_rows, (1, present_adapters)), jnp.zeros((), jnp.bfloat16)
    )
    adapter_correction = jnp.dot(
        expanded_rows, up_matrix, preferred_element_type=jnp.float32
    ).astype(jnp.bfloat16)
    adapter_correction = adapter_correction.reshape(source_rows, entry_list, column_portion)
    returned_rows = lax.all_to_all(
        adapter_correction, "wide", split_axis=0, concat_axis=0, tiled=True
    )
    returned_rows = returned_rows.reshape(wide_count * capacity, column_portion)
    adapter_row_output = returned_rows[storage_slot_index]
    return (base_projection_output + adapter_row_output.astype(jnp.float32)).astype(jnp.bfloat16)


def solution(mesh):
    in_specs = (
        P("wide", "tensor"),
        P(None, "tensor"),
        P("tensor", "wide", None),
        P("wide", None, "tensor"),
        P("wide"),
        P(),
    )
    out_specs = P("wide", "tensor")
    return jax.shard_map(body, mesh=mesh, in_specs=in_specs, out_specs=out_specs, check_vma=False)
```

profile of v0, /device:TPU:24, one launch (start us, length us, event | category | flops | bytes accessed | tf_op | source)
XLA Modules:
  0.0 157.6 jit_solution(14151198750834206589)
XLA Ops:
  6.5 0.0 copy-start
  6.5 0.0 all-gather.2.cloned.1.call-start
  6.5 0.7 all-gather.2.cloned.1.call-update
  7.3 0.9 select_reduce_fusion
  8.2 1.2 reduce-window.6
  9.4 0.2 slice_reduce_fusion
  9.7 0.1 fusion.12
  9.8 2.4 %scatter_custom_fusion = s32[1024]{0:T(1024)S(1)} fusion(s32[512]{0:T(512)S(1)} %bitcast.57, s32[512]{0:T(512)S(1)} %get-tuple-element.5, s32[]{:T(128)} %constant.50.clone.1), kind=kCustom, calls=%fused_computation.59 | custom fusion | bytes 4100 | tf_op jit(solution)/shard_map/scatter | solution.py:41
  12.3 0.7 all_to_all.12
  13.0 13.2 %all-to-all-start = ((s32[32,1,32]{2,1,0:T(1,128)}), s32[32,1,32]{2,1,0:T(1,128)S(1)}, u32[]{:S(2)}, u32[]{:S(2)}) async-start(s32[32,1,32]{2,1,0:T(1,128)} %all_to_all.12), calls=%async_computation | async-start | bytes 32768 | tf_op jit(solution)/shard_map/all_to_all | solution.py:51
  26.1 4.1 %scatter_custom_fusion.1 = bf16[1024,512]{1,0:T(8,128)(2,1)} fusion(s32[512]{0:T(512)S(1)} %bitcast.58, bf16[512,512]{1,0:T(8,128)(2,1)} %param.6, bf16[]{:T(256)} %constant.61.clone.1), kind=kCustom, calls=%fused_computation.16 | custom fusion | bytes 1049088 | tf_op jit(solution)/shard_map/scatter | solution.py:38
  30.2 5.6 %all-to-all-done = s32[32,1,32]{2,1,0:T(1,128)S(1)} async-done(((s32[32,1,32]{2,1,0:T(1,128)}), s32[32,1,32]{2,1,0:T(1,128)S(1)}, u32[]{:S(2)}, u32[]{:S(2)}) %all-to-all-start) | async-done | bytes 4128 | tf_op jit(solution)/shard_map/all_to_all | solution.py:51
  35.8 4.2 %all-to-all-start.1 = ((bf16[32,32,512]{2,1,0:T(8,128)(2,1)}), bf16[32,32,512]{2,1,0:T(8,128)(2,1)S(1)}, u32[]{:S(2)}, u32[]{:S(2)}) async-start(bf16[32,32,512]{2,1,0:T(8,128)(2,1)} %bitcast.5), calls=%async_computation.1 | async-start | bytes 2097152 | tf_op jit(solution)/shard_map/all_to_all | solution.py:50
  40.0 0.5 broadcast.228
  40.5 0.7 reduce.5
  41.2 0.1 eq.71
  41.3 26.2 %all-to-all-done.1 = bf16[32,32,512]{2,1,0:T(8,128)(2,1)S(1)} async-done(((bf16[32,32,512]{2,1,0:T(8,128)(2,1)}), bf16[32,32,512]{2,1,0:T(8,128)(2,1)S(1)}, u32[]{:S(2)}, u32[]{:S(2)}) %all-to-all-start.1) | async-done | bytes 1048608 | tf_op jit(solution)/shard_map/all_to_all | solution.py:50
  67.5 4.5 %compare_select_fusion = f32[1024,1024]{0,1:T(8,128)} fusion(bf16[1024,512]{1,0:T(8,128)(2,1)S(1)} %bitcast.55, bf16[512,1024]{0,1:T(8,128)(2,1)} %bitcast.61, s32[1024]{0:T(1024)S(1)} %eq.71, s32[1024]{0:T(1024)S(1)} %add_select_fusion.1), kind=kOutput, calls=%fused_computation.3 | convolution fusion | flops 1075838976 | bytes 6299648 | tf_op jit(solution)/shard_map/dot_general | solution.py:55
  71.9 0.0 copy-start.1
  72.0 2.5 %reduce_sum.38 = f32[1024,64]{0,1:T(8,128)S(1)} reduce(f32[1024,16,64]{0,2,1:T(8,128)} %bitcast.54, f32[]{:T(128)} %constant.62.clone.1), dimensions={1}, to_apply=%region_6.7 | reduce | flops 983040 | bytes 4456452 | tf_op jit(solution)/shard_map/reduce_sum | solution.py:57
  74.5 47.2 %all-reduce.1 = bf16[1024,64]{0,1:T(8,128)(2,1)S(1)} all-reduce(f32[1024,64]{0,1:T(8,128)S(1)} %reduce_sum.38), channel_id=1, replica_groups=mesh['wide'=32,'tensor'=16] {'tensor'}, use_global_device_ids=true, to_apply=%region_7.8 | all-reduce | flops 65536 | bytes 393216 | tf_op jit(solution)/shard_map/psum | solution.py:63
  121.7 0.0 copy-done.1
  121.7 1.7 %fusion.4 = bf16[1024,128]{1,0:T(8,128)(2,1)} fusion(bf16[16,64,128]{2,1,0:T(8,128)(2,1)S(1)} %copy-done.1, s32[16,64]{1,0:T(8,128)S(1)} %add_select_fusion, s32[1024]{0:T(1024)S(1)} %eq.71, bf16[1024,64]{0,1:T(8,128)(2,1)S(1)} %all-reduce.1), kind=kOutput, calls=%fused_computation.9 | convolution fusion | flops 270663680 | bytes 663552 | tf_op jit(solution)/shard_map/dot_general | solution.py:68
  123.4 5.7 %all-to-all-start.2 = ((bf16[32,32,128]{2,1,0:T(8,128)(2,1)}), bf16[32,32,128]{2,1,0:T(8,128)(2,1)S(1)}, u32[]{:S(2)}, u32[]{:S(2)}) async-start(bf16[32,32,128]{2,1,0:T(8,128)(2,1)} %bitcast.10), calls=%async_computation.2 | async-start | bytes 524288 | tf_op jit(solution)/shard_map/all_to_all | solution.py:72
  129.1 13.9 %all-to-all-done.2 = bf16[32,32,128]{2,1,0:T(8,128)(2,1)S(1)} async-done(((bf16[32,32,128]{2,1,0:T(8,128)(2,1)}), bf16[32,32,128]{2,1,0:T(8,128)(2,1)S(1)}, u32[]{:S(2)}, u32[]{:S(2)}) %all-to-all-start.2) | async-done | bytes 262176 | tf_op jit(solution)/shard_map/all_to_all | solution.py:72
  143.0 1.3 gather_fusion
  144.3 0.0 all-gather.2.cloned.1.call-done
  144.4 0.0 copy-done
  144.4 6.4 %fusion.5 = bf16[512,128]{1,0:T(8,128)(2,1)} fusion(bf16[512,8192]{1,0:T(8,128)(2,1)} %all-gather.2.cloned.1.call-done, bf16[8192,128]{1,0:T(8,128)(2,1)S(1)} %copy-done, bf16[512,128]{1,0:T(8,128)(2,1)S(1)} %gather_fusion), kind=kOutput, calls=%fused_computation.11 | convolution fusion | flops 1073938432 | bytes 10747904 | tf_op jit(solution)/shard_map/dot_general | solution.py:23
  (9 shorter events, 0.1 us)
Async XLA Ops:
  6.5 137.8 %copy-start = (bf16[8192,128]{1,0:T(8,128)(2,1)S(1)}, bf16[8192,128]{1,0:T(8,128)(2,1)}, u32[]{:S(2)}) copy-start(bf16[8192,128]{1,0:T(8,128)(2,1)} %param.7) | copy-start | bytes 6291460
  6.5 137.8 %all-gather.2.cloned.1.call-start = ((), (), s32[]{:S(2)}) async-start(), calls=%async_computation.3 | async-start | bytes 8912896 | tf_op jit(solution)/shard_map/all_gather | solution.py:22
  13.0 22.8 %all-to-all-start = ((s32[32,1,32]{2,1,0:T(1,128)}), s32[32,1,32]{2,1,0:T(1,128)S(1)}, u32[]{:S(2)}, u32[]{:S(2)}) async-start(s32[32,1,32]{2,1,0:T(1,128)} %all_to_all.12), calls=%async_computation | async-start | bytes 32768 | tf_op jit(solution)/shard_map/all_to_all | solution.py:51
  35.8 31.7 %all-to-all-start.1 = ((bf16[32,32,512]{2,1,0:T(8,128)(2,1)}), bf16[32,32,512]{2,1,0:T(8,128)(2,1)S(1)}, u32[]{:S(2)}, u32[]{:S(2)}) async-start(bf16[32,32,512]{2,1,0:T(8,128)(2,1)} %bitcast.5), calls=%async_computation.1 | async-start | bytes 2097152 | tf_op jit(solution)/shard_map/all_to_all | solution.py:50
  71.9 49.7 %copy-start.1 = (bf16[16,64,128]{2,1,0:T(8,128)(2,1)S(1)}, bf16[16,64,128]{2,1,0:T(8,128)(2,1)}, u32[]{:S(2)}) copy-start(bf16[16,64,128]{2,1,0:T(8,128)(2,1)} %param.9) | copy-start | bytes 786436
  123.4 19.6 %all-to-all-start.2 = ((bf16[32,32,128]{2,1,0:T(8,128)(2,1)}), bf16[32,32,128]{2,1,0:T(8,128)(2,1)S(1)}, u32[]{:S(2)}, u32[]{:S(2)}) async-start(bf16[32,32,128]{2,1,0:T(8,128)(2,1)} %bitcast.10), calls=%async_computation.2 | async-start | bytes 524288 | tf_op jit(solution)/shard_map/all_to_all | solution.py:72
Sparse Core Ops, SparseCore 0:
  9.5 62.3 all-gather.1
where the time goes:
time: 158 us
  blocking collectives  47.2 us (30%)
  waiting for transfers between devices  46.4 us (29%)
  starting transfers between devices  23 us (15%)
  between operations  13.5 us (9%)
  matrix products  12.6 us (8%)
  local copies, waits for them, and re-layouts  9.34 us (6%)
  other arithmetic  5.53 us (4%)
    psum x1, blocking collectives, body(): summed = lax.psum(partial_value, 'tensor')  47.2 us
    all_to_all x1, waiting for transfers between devices, body(): lax.all_to_all(send_rows, 'wide', split_axis=0, concat_axis=0, tiled=True)  26.2 us
    all_to_all x1, waiting for transfers between devices, body(): lax.all_to_all(adapter_correction, 'wide', split_axis=0, concat_axis=0, t...  13.9 us
    all_to_all x1, starting transfers between devices, body(): lax.all_to_all(send_slots, 'wide', split_axis=0, concat_axis=0, tiled=True)  13.2 us
    dot_general x1, matrix products, body(): jnp.dot(gathered, key_value_weight, preferred_element_type=jnp.float32)  6.39 us
    all_to_all x1, starting transfers between devices, body(): lax.all_to_all(adapter_correction, 'wide', split_axis=0, concat_axis=0, t...  5.67 us
    all_to_all x1, waiting for transfers between devices, body(): lax.all_to_all(send_slots, 'wide', split_axis=0, concat_axis=0, tiled=True)  5.61 us
    dot_general x1, matrix products, body(): jnp.dot(flat_rows, down_matrix, preferred_element_type=jnp.float32)  4.49 us
  transfers between devices with their start and end apart: 4, of which 3 were waited for; matrix products, arithmetic and copies ran while one was open for 13% of the time, Pallas kernels for 0%

commit v1 on v0

--- a/solution.py
+++ b/solution.py
@@ -2,6 +2,12 @@
 import jax.numpy as jnp
 from jax import lax
 from jax.sharding import PartitionSpec as P
+
+
+def gather_and_add(x, axis):
+    parts = lax.all_gather(x, axis, axis=0, tiled=False)
+    total = parts.sum(axis=0)
+    return total
 
 
 def body(
@@ -60,7 +66,7 @@
         ),
         axis=1,
     )
-    summed = lax.psum(partial_value, "tensor")
+    summed = gather_and_add(partial_value, "tensor")
     reduced_rows = summed.astype(jnp.bfloat16)
     expanded_rows = jnp.where(
         selected, jnp.tile(reduced_rows, (1, present_adapters)), jnp.zeros((), jnp.bfloat16)

time: 158 us -> 191 us (1.21)
  the two profiles are of different devices: /device:TPU:24 before, /device:TPU:1 now
where the time goes in v1:
time: 191 us; the launch traced here: 190 us
  waiting for transfers between devices  115 us (60%)
  starting transfers between devices  28.6 us (15%)
  local copies, waits for them, and re-layouts  13.9 us (7%)
  between operations  13.5 us (7%)
  matrix products  12.5 us (7%)
  other arithmetic  7.17 us (4%)
    all_gather x1, waiting for transfers between devices, gather_and_add(): parts = lax.all_gather(x, axis, axis=0, tiled=False)  44.2 us
    all_gather x1, waiting for transfers between devices, body(): gathered = lax.all_gather(tokens, 'tensor', axis=1, tiled=True)  29.4 us
    all_to_all x1, waiting for transfers between devices, body(): lax.all_to_all(send_rows, 'wide', split_axis=0, concat_axis=0, tiled=True)  24.3 us
    all_to_all x1, starting transfers between devices, body(): lax.all_to_all(send_slots, 'wide', split_axis=0, concat_axis=0, tiled=True)  13.7 us
    all_to_all x1, waiting for transfers between devices, body(): lax.all_to_all(adapter_correction, 'wide', split_axis=0, concat_axis=0, t...  11.5 us
    all_to_all x1, starting transfers between devices, body(): lax.all_to_all(adapter_correction, 'wide', split_axis=0, concat_axis=0, t...  10.1 us
    dot_general x1, matrix products, body(): jnp.dot(gathered, key_value_weight, preferred_element_type=jnp.float32)  6.39 us
    all_to_all x1, starting transfers between devices, body(): lax.all_to_all(send_rows, 'wide', split_axis=0, concat_axis=0, tiled=True)  4.68 us
  transfers between devices with their start and end apart: 5, of which 5 were waited for; matrix products, arithmetic and copies ran while one was open for 7% of the time, Pallas kernels for 0%

profile of v1, /device:TPU:1, one launch (start us, length us, event | category | flops | bytes accessed | tf_op | source)
XLA Modules:
  0.0 190.4 jit_solution(4802829308427890857)
XLA Ops:
  6.5 0.0 copy-start
  6.5 1.1 select_reduce_fusion
  7.7 1.2 reduce-window.6
  8.8 0.2 slice_reduce_fusion
  9.1 0.1 fusion.12
  9.2 2.4 %scatter_custom_fusion = s32[1024]{0:T(1024)S(1)} fusion(s32[512]{0:T(512)S(1)} %bitcast.63, s32[512]{0:T(512)S(1)} %get-tuple-element.5, s32[]{:T(128)} %constant.50.clone.1), kind=kCustom, calls=%fused_computation.60 | custom fusion | bytes 4100 | tf_op jit(solution)/shard_map/scatter | solution.py:47
  11.7 0.7 all_to_all.12
  12.4 13.7 %all-to-all-start = ((s32[32,1,32]{2,1,0:T(1,128)}), s32[32,1,32]{2,1,0:T(1,128)S(1)}, u32[]{:S(2)}, u32[]{:S(2)}) async-start(s32[32,1,32]{2,1,0:T(1,128)} %all_to_all.12), calls=%async_computation | async-start | bytes 32768 | tf_op jit(solution)/shard_map/all_to_all | solution.py:57
  26.1 4.0 %scatter_custom_fusion.1 = bf16[1024,512]{1,0:T(8,128)(2,1)} fusion(s32[512]{0:T(512)S(1)} %bitcast.64, bf16[512,512]{1,0:T(8,128)(2,1)} %param.6, bf16[]{:T(256)} %constant.61.clone.1), kind=kCustom, calls=%fused_computation.17 | custom fusion | bytes 1049088 | tf_op jit(solution)/shard_map/scatter | solution.py:44
  30.1 4.5 %all-to-all-done = s32[32,1,32]{2,1,0:T(1,128)S(1)} async-done(((s32[32,1,32]{2,1,0:T(1,128)}), s32[32,1,32]{2,1,0:T(1,128)S(1)}, u32[]{:S(2)}, u32[]{:S(2)}) %all-to-all-start) | async-done | bytes 4128 | tf_op jit(solution)/shard_map/all_to_all | solution.py:57
  34.6 4.7 %all-to-all-start.1 = ((bf16[32,32,512]{2,1,0:T(8,128)(2,1)}), bf16[32,32,512]{2,1,0:T(8,128)(2,1)S(1)}, u32[]{:S(2)}, u32[]{:S(2)}) async-start(bf16[32,32,512]{2,1,0:T(8,128)(2,1)} %bitcast.5), calls=%async_computation.1 | async-start | bytes 2097152 | tf_op jit(solution)/shard_map/all_to_all | solution.py:56
  39.3 0.0 all-gather.6.cloned.1.call-start
  39.4 0.5 broadcast.228
  39.9 0.7 reduce.5
  40.6 0.1 eq.71
  40.7 24.3 %all-to-all-done.1 = bf16[32,32,512]{2,1,0:T(8,128)(2,1)S(1)} async-done(((bf16[32,32,512]{2,1,0:T(8,128)(2,1)}), bf16[32,32,512]{2,1,0:T(8,128)(2,1)S(1)}, u32[]{:S(2)}, u32[]{:S(2)}) %all-to-all-start.1) | async-done | bytes 1048608 | tf_op jit(solution)/shard_map/all_to_all | solution.py:56
  65.0 4.4 %compare_select_fusion = f32[1024,1024]{0,1:T(8,128)} fusion(bf16[1024,512]{1,0:T(8,128)(2,1)S(1)} %bitcast.61, bf16[512,1024]{0,1:T(8,128)(2,1)} %bitcast.67, s32[1024]{0:T(1024)S(1)} %eq.71, s32[1024]{0:T(1024)S(1)} %add_select_fusion.1), kind=kOutput, calls=%fused_computation.4 | convolution fusion | flops 1075838976 | bytes 6299648 | tf_op jit(solution)/shard_map/dot_general | solution.py:61
  69.4 3.2 %reduce_sum.47 = f32[1024,64]{0,1:T(8,128)} reduce(f32[1024,16,64]{0,2,1:T(8,128)} %bitcast.59, f32[]{:T(128)} %constant.62.clone.1), dimensions={1}, to_apply=%region_6.7 | reduce | flops 983040 | bytes 4456452 | tf_op jit(solution)/shard_map/reduce_sum | solution.py:63
  72.6 0.0 all-gather.6.cloned.1.call-update
  72.6 0.0 all-gather.4.cloned.1.call-start
  72.7 0.7 all-gather.4.cloned.1.call-update
  73.4 44.2 %all-gather.6.cloned.1.call-done = f32[16384,64]{0,1:T(8,128)} async-done(((f32[1024,64]{0,1:T(8,128)}), f32[16384,64]{0,1:T(8,128)}) %all-gather.6.cloned.1.call-update) | async-done | bytes 4194320 | tf_op jit(solution)/shard_map/all_gather | solution.py:8
  117.6 4.6 %copy.11 = f32[8,8,16,1024]{3,2,1,0:T(8,128)S(1)} copy(f32[8,8,16,1024]{3,1,2,0:T(8,128)} %bitcast.60) | data formatting | bytes 8388608
  122.1 0.0 copy-start.1
  122.1 0.8 bitcast_reduce_fusion
  123.0 0.1 copy-done.1
  123.1 1.7 fusion.4
  124.8 10.1 %all-to-all-start.2 = ((bf16[32,32,128]{2,1,0:T(8,128)(2,1)}), bf16[32,32,128]{2,1,0:T(8,128)(2,1)S(1)}, u32[]{:S(2)}, u32[]{:S(2)}) async-start(bf16[32,32,128]{2,1,0:T(8,128)(2,1)} %bitcast.10), calls=%async_computation.2 | async-start | bytes 524288 | tf_op jit(solution)/shard_map/all_to_all | solution.py:78
  134.9 11.5 %all-to-all-done.2 = bf16[32,32,128]{2,1,0:T(8,128)(2,1)S(1)} async-done(((bf16[32,32,128]{2,1,0:T(8,128)(2,1)}), bf16[32,32,128]{2,1,0:T(8,128)(2,1)S(1)}, u32[]{:S(2)}, u32[]{:S(2)}) %all-to-all-start.2) | async-done | bytes 262176 | tf_op jit(solution)/shard_map/all_to_all | solution.py:78
  146.4 1.3 gather_fusion
  147.7 29.4 %all-gather.4.cloned.1.call-done = bf16[512,8192]{1,0:T(8,128)(2,1)} async-done(((bf16[512,512]{1,0:T(8,128)(2,1)}), bf16[512,8192]{1,0:T(8,128)(2,1)}) %all-gather.4.cloned.1.call-update) | async-done | bytes 8388624 | tf_op jit(solution)/shard_map/all_gather | solution.py:28
  177.1 0.0 copy-done
  177.1 6.4 %fusion.5 = bf16[512,128]{1,0:T(8,128)(2,1)} fusion(bf16[512,8192]{1,0:T(8,128)(2,1)} %all-gather.4.cloned.1.call-done, bf16[8192,128]{1,0:T(8,128)(2,1)S(1)} %copy-done, bf16[512,128]{1,0:T(8,128)(2,1)S(1)} %gather_fusion), kind=kOutput, calls=%fused_computation.12 | convolution fusion | flops 1073938432 | bytes 10747904 | tf_op jit(solution)/shard_map/dot_general | solution.py:29
  (9 shorter events, 0.1 us)
Async XLA Ops:
  6.5 170.6 %copy-start = (bf16[8192,128]{1,0:T(8,128)(2,1)S(1)}, bf16[8192,128]{1,0:T(8,128)(2,1)}, u32[]{:S(2)}) copy-start(bf16[8192,128]{1,0:T(8,128)(2,1)} %param.7) | copy-start | bytes 6291460
  12.4 22.2 %all-to-all-start = ((s32[32,1,32]{2,1,0:T(1,128)}), s32[32,1,32]{2,1,0:T(1,128)S(1)}, u32[]{:S(2)}, u32[]{:S(2)}) async-start(s32[32,1,32]{2,1,0:T(1,128)} %all_to_all.12), calls=%async_computation | async-start | bytes 32768 | tf_op jit(solution)/shard_map/all_to_all | solution.py:57
  34.6 30.4 %all-to-all-start.1 = ((bf16[32,32,512]{2,1,0:T(8,128)(2,1)}), bf16[32,32,512]{2,1,0:T(8,128)(2,1)S(1)}, u32[]{:S(2)}, u32[]{:S(2)}) async-start(bf16[32,32,512]{2,1,0:T(8,128)(2,1)} %bitcast.5), calls=%async_computation.1 | async-start | bytes 2097152 | tf_op jit(solution)/shard_map/all_to_all | solution.py:56
  39.3 78.2 %all-gather.6.cloned.1.call-start = ((), (), s32[]{:S(2)}) async-start(), calls=%async_computation.4 | async-start | bytes 4456448 | tf_op jit(solution)/shard_map/all_gather | solution.py:8
  72.6 104.5 %all-gather.4.cloned.1.call-start = ((), (), s32[]{:S(2)}) async-start(), calls=%async_computation.3 | async-start | bytes 8912896 | tf_op jit(solution)/shard_map/all_gather | solution.py:28
  122.1 1.0 copy-start.1
  124.8 21.6 %all-to-all-start.2 = ((bf16[32,32,128]{2,1,0:T(8,128)(2,1)}), bf16[32,32,128]{2,1,0:T(8,128)(2,1)S(1)}, u32[]{:S(2)}, u32[]{:S(2)}) async-start(bf16[32,32,128]{2,1,0:T(8,128)(2,1)} %bitcast.10), calls=%async_computation.2 | async-start | bytes 524288 | tf_op jit(solution)/shard_map/all_to_all | solution.py:78
Sparse Core Ops, SparseCore 0:
  72.8 44.7 all-gather.5
  119.7 57.3 all-gather.3
